TPU v7x, 128 devices: a whole 4x4x4 slice. The times are simulated.
128 devices in a mesh: wide: 16 (over z, y), col: 8 (over x, core).
Axes of the slice: x: 4, y: 4, z: 4, core: 2. Of those that a mesh axis runs over, the one named last changes fastest.
Arguments:
- z_root: float32 [512, 16384], P('col', 'wide'), may hold values from -6 to 6
- z_child: float32 [512, 2, 8192], P('col', None, 'wide'), may hold values from -6 to 6
- z_grand: float32 [512, 4, 4096], P('col', None, 'wide'), may hold values from -6 to 6
- inv_root: float32 [16384, 16384], P('wide', 'col'), as said below
- inv_child: float32 [2, 8192, 8192], P(None, 'wide', 'col'), as said below
- inv_grand: float32 [4, 4096, 4096], P(None, 'wide', 'col'), as said below
- panel_child: float32 [2, 4096, 8192], P(None, 'col', 'wide'), may hold values from -0.046875 to 0.046875
- panel_grand: float32 [4, 2048, 4096], P(None, 'col', 'wide'), may hold values from -0.0625 to 0.0625
- anc_child: int32 [2, 32], P(None, 'col'), may hold values from 0 to 127, as said below
- anc_grand: int32 [4, 16], P(None, 'col'), may hold values from 0 to 255, as said below
Outputs:
- x_root: float32 [512, 16384], P('wide', 'col')
- x_child: float32 [512, 2, 8192], P('wide', None, 'col')
- x_grand: float32 [512, 4, 4096], P('wide', None, 'col')
Inputs may be any that keep to these rules, and one draw needn't show every extreme that they name: inv_root is lower triangular with a positive diagonal (entries above the diagonal are zero). Each inv_child[k] is lower triangular with a positive diagonal. Each inv_grand[g] is lower triangular with a positive diagonal. `anc_child`: each row lists distinct blocks in rising order and always names block 0 and block 127. `anc_grand`: row g lists 2048 // 256 distinct root blocks in rising order, block 0 and block 127 among them, then as many distinct blocks of child g // 2 (numbered 16384 // 128 + (g // 2) * 64 onwards) in rising order, its first and its last among them.
All inputs are finite; a program needn't handle non-finite values.
Results may differ from a plain program's by a relative error of at most 0.000096.
Values sent between devices are 32-bit elements; how exact they have to be, the bound alone decides.
No kernel may reach another device: no remote copies, remote signals or barrier semaphores. Data moves between devices by JAX's collectives and lax.ppermute only.
A program may use at most 128 MiB of HBM per device.

v0:
```python
import jax
import jax.numpy as jnp
from jax import lax
from jax.sharding import PartitionSpec as P

BLK = 128
PRECISE = lax.Precision.HIGHEST


def pick_blocks(source_rows, blocks):
    leading = source_rows.shape[0]
    tiled = source_rows.reshape(leading, source_rows.shape[1] // BLK, BLK)
    selected = jnp.take(tiled, blocks.reshape(-1), axis=1)
    return selected.reshape(leading, blocks.shape[0], blocks.shape[1] * BLK)


def spread_rhs(local_part):
    return lax.all_gather(local_part, "col", axis=0, tiled=True)


def solve_terms(right_rows, inverse):
    return lax.psum_scatter(
        jnp.einsum(
            "ski,kij->skj",
            right_rows,
            inverse,
            precision=PRECISE,
            preferred_element_type=jnp.float32,
        ),
        "wide",
        scatter_dimension=0,
        tiled=True,
    )


def spread_solved(solved_local):
    gathered = lax.all_gather(solved_local, "col", axis=2, tiled=True)
    return gathered.reshape(gathered.shape[0], -1)


def fetch_ancestors(source_rows, blocks):
    return lax.all_gather(pick_blocks(source_rows, blocks), "wide", axis=0, tiled=True)


def finish_level(z_local, inverse, partial_value):
    summed = lax.psum(partial_value, "col")
    right_side = spread_rhs(z_local) - summed
    solved = solve_terms(right_side, inverse)
    return solved


def per_device(
    z_root,
    z_child,
    z_grand,
    inv_root,
    inv_child,
    inv_grand,
    panel_child,
    panel_grand,
    anc_child,
    anc_grand,
):
    root_right = spread_rhs(z_root[:, None, :])
    root_solved = solve_terms(root_right, inv_root[None])
    x_root = root_solved[:, 0, :]
    root_rows = spread_solved(root_solved)
    near_rows = fetch_ancestors(root_rows, anc_child)
    partial_value = jnp.einsum(
        "ska,kaj->skj",
        near_rows,
        panel_child,
        precision=PRECISE,
        preferred_element_type=jnp.float32,
    )
    x_child = finish_level(z_child, inv_child, partial_value)
    child_rows = spread_solved(x_child)
    solved_all = jnp.concatenate([root_rows, child_rows], axis=1)
    far_rows = fetch_ancestors(solved_all, anc_grand)
    partial_grand = jnp.einsum(
        "sga,gaj->sgj", far_rows, panel_grand, precision=PRECISE, preferred_element_type=jnp.float32
    )
    x_grand = finish_level(z_grand, inv_grand, partial_grand)
    return (x_root, x_child, x_grand)


def solution(mesh):
    in_specs = (
        P("col", "wide"),
        P("col", None, "wide"),
        P("col", None, "wide"),
        P("wide", "col"),
        P(None, "wide", "col"),
        P(None, "wide", "col"),
        P(None, "col", "wide"),
        P(None, "col", "wide"),
        P(None, "col"),
        P(None, "col"),
    )
    out_specs = (P("wide", "col"), P("wide", None, "col"), P("wide", None, "col"))
    return jax.shard_map(
        per_device, mesh=mesh, in_specs=in_specs, out_specs=out_specs, check_vma=False
    )
```

profile of v0, /device:TPU:0, one launch (start us, length us, event | category | flops | bytes accessed | tf_op | source)
XLA Modules:
  0.0 726.2 jit_solution(2255232434404925078)
XLA Ops:
  7.2 0.7 all-gather.21.cloned.1.call-update
  8.0 29.4 %all-gather.21.cloned.1.call-done = f32[512,1024]{1,0:T(8,128)} async-done(((f32[64,1024]{1,0:T(8,128)}), f32[512,1024]{1,0:T(8,128)}) %all-gather.21.cloned.1.call-update) | async-done | bytes 2097168 | tf_op jit(solution)/shard_map/all_gather | solution.py:18
  37.4 30.4 %convolution_bitcast_fusion = f32[512,1,2048]{0,2,1:T(8,128)} fusion(f32[1024,2048]{1,0:T(8,128)} %param.13, f32[512,1024]{1,0:T(8,128)} %all-gather.21.cloned.1.call-done), kind=kOutput, calls=%fused_computation.3 | convolution fusion | flops 12884901888 | bytes 14680064 | tf_op jit(solution)/shard_map/ski,kij->skj/dot_general | solution.py:23
  67.8 11.0 %copy.75 = f32[512,1,2048]{2,1,0:T(1,128)} copy(f32[512,1,2048]{0,2,1:T(8,128)} %convolution_bitcast_fusion) | data formatting | bytes 8388608 | tf_op jit(solution)/shard_map/ski,kij->skj/transpose | solution.py:23
  78.8 0.0 all-gather.11.cloned.1.call-start
  78.9 0.6 copy-done.8
  79.5 0.6 dynamic-slice
  80.7 102.2 %all-reduce.9.cloned.1.call-done = f32[512,1,2048]{2,1,0:T(1,128)} async-done(((f32[512,1,2048]{2,1,0:T(1,128)}), f32[512,1,2048]{2,1,0:T(1,128)}) %all-reduce.9.cloned.1.call-update) | async-done | bytes 4194320
  183.0 1.7 constant_dynamic-slice_fusion
  184.7 0.1 reshape.104
  184.8 0.1 broadcast_bitcast_fusion.1
  184.9 25.1 %all-gather.11.cloned.1.call-done = f32[32,1,16384]{2,1,0:T(1,128)} async-done(((f32[32,1,2048]{2,1,0:T(1,128)}), f32[32,1,16384]{2,1,0:T(1,128)}) %all-gather.11.cloned.1.call-update) | async-done | bytes 2097168 | tf_op jit(solution)/shard_map/all_gather | solution.py:37
  210.0 4.2 copy.77
  214.3 2.1 gather_fusion
  216.4 0.1 copy.78
  216.5 0.1 gather.13
  216.6 0.7 copy_select_fusion.1
  217.3 0.8 copy.76
  218.1 0.0 all-reduce.5.cloned.1.call-start
  218.2 44.9 %all-gather.13.cloned.1.call-done = f32[512,2,512]{2,0,1:T(8,128)} async-done(((f32[32,2,512]{2,0,1:T(8,128)}), f32[512,2,512]{2,0,1:T(8,128)}) %all-gather.13.cloned.1.call-update) | async-done | bytes 2097168 | tf_op jit(solution)/shard_map/all_gather | solution.py:42
  263.0 7.0 convolution_bitcast_fusion.4
  270.1 19.4 %all-gather.9.cloned.1.call-done = f32[512,2,512]{2,0,1:T(8,128)} async-done(((f32[64,2,512]{2,0,1:T(8,128)}), f32[512,2,512]{2,0,1:T(8,128)}) %all-gather.9.cloned.1.call-update) | async-done | bytes 2097168 | tf_op jit(solution)/shard_map/all_gather | solution.py:18
  289.6 68.2 %all-reduce.5.cloned.1.call-done = f32[512,2,512]{2,0,1:T(8,128)} async-done(((f32[512,2,512]{2,0,1:T(8,128)}), f32[512,2,512]{2,0,1:T(8,128)}) %all-reduce.5.cloned.1.call-update) | async-done | bytes 2097168 | tf_op jit(solution)/shard_map/psum | solution.py:46
  357.8 12.2 %convolution_bitcast_fusion.2 = f32[512,2,1024]{2,0,1:T(8,128)} fusion(f32[2,512,1024]{2,1,0:T(8,128)} %param.14, f32[512,2,512]{2,0,1:T(8,128)} %all-gather.9.cloned.1.call-done, f32[512,2,512]{2,0,1:T(8,128)} %all-reduce.5.cloned.1.call-done), kind=kOutput, calls=%fused_computation.5 | convolution fusion | flops 6442975232 | bytes 12582912 | tf_op jit(solution)/shard_map/ski,kij->skj/dot_general | solution.py:23
  370.1 77.5 %reduce-scatter.3.cloned.1.call-done = f32[32,2,1024]{2,0,1:T(8,128)} async-done(((f32[512,2,1024]{2,0,1:T(8,128)}), f32[32,2,1024]{2,0,1:T(8,128)}) %reduce-scatter.3.cloned.1.call-update) | async-done | bytes 262160 | tf_op jit(solution)/shard_map/reduce_scatter | solution.py:22
  447.6 0.1 copy.84
  447.7 0.1 reshape.105
  447.9 0.1 broadcast_bitcast_fusion
  447.9 25.8 %all-gather.17.cloned.1.call-done = f32[32,2,8192]{2,0,1:T(8,128)} async-done(((f32[32,2,1024]{2,0,1:T(8,128)}), f32[32,2,8192]{2,0,1:T(8,128)}) %all-gather.17.cloned.1.call-update) | async-done | bytes 2097168 | tf_op jit(solution)/shard_map/all_gather | solution.py:37
  473.7 4.6 copy.81
  478.3 4.0 concatenate.6
  482.3 3.0 copy.83
  485.3 2.4 pad_maximum_fusion
  487.7 2.8 gather_fusion.1
  490.5 0.1 copy.85
  490.6 0.1 gather.15
  490.7 0.7 copy_select_fusion
  491.4 1.7 copy.80
  493.2 43.9 %all-gather.19.cloned.1.call-done = f32[512,4,256]{2,0,1:T(8,128)} async-done(((f32[32,4,256]{2,0,1:T(8,128)}), f32[512,4,256]{2,0,1:T(8,128)}) %all-gather.19.cloned.1.call-update) | async-done | bytes 2097168 | tf_op jit(solution)/shard_map/all_gather | solution.py:42
  537.1 4.9 convolution_bitcast_fusion.3
  542.1 21.7 %all-gather.15.cloned.1.call-done = f32[512,4,256]{2,0,1:T(8,128)} async-done(((f32[64,4,256]{2,0,1:T(8,128)}), f32[512,4,256]{2,0,1:T(8,128)}) %all-gather.15.cloned.1.call-update) | async-done | bytes 2097168 | tf_op jit(solution)/shard_map/all_gather | solution.py:18
  563.8 68.5 %all-reduce.7.cloned.1.call-done = f32[512,4,256]{2,0,1:T(8,128)} async-done(((f32[512,4,256]{2,0,1:T(8,128)}), f32[512,4,256]{2,0,1:T(8,128)}) %all-reduce.7.cloned.1.call-update) | async-done | bytes 2097168 | tf_op jit(solution)/shard_map/psum | solution.py:46
  632.3 7.8 %convolution_bitcast_fusion.1 = f32[512,4,512]{2,0,1:T(8,128)} fusion(f32[4,256,512]{2,1,0:T(8,128)S(1)} %copy-done, f32[512,4,256]{2,0,1:T(8,128)} %all-gather.15.cloned.1.call-done, f32[512,4,256]{2,0,1:T(8,128)} %all-reduce.7.cloned.1.call-done), kind=kOutput, calls=%fused_computation.4 | convolution fusion | flops 3221749760 | bytes 10485760 | tf_op jit(solution)/shard_map/ski,kij->skj/dot_general | solution.py:23
  640.0 0.9 copy-done.2
  641.0 0.8 copy.95
  641.8 0.9 copy.87
  642.7 74.9 %reduce-scatter.5.cloned.1.call-done = f32[32,4,512]{2,0,1:T(8,128)} async-done(((f32[512,4,512]{2,0,1:T(8,128)}), f32[32,4,512]{2,0,1:T(8,128)}) %reduce-scatter.5.cloned.1.call-update) | async-done | bytes 262160 | tf_op jit(solution)/shard_map/reduce_scatter | solution.py:22
  717.6 1.8 copy.88
  (44 shorter events, 0.7 us)
Async XLA Ops:
  7.2 625.1 %copy-start = (f32[4,256,512]{2,1,0:T(8,128)S(1)}, f32[4,256,512]{2,1,0:T(8,128)}, u32[]{:S(2)}) copy-start(f32[4,256,512]{2,1,0:T(8,128)} %param.15) | copy-start | bytes 6291460
  7.2 30.2 %all-gather.21.cloned.1.call-start = ((), (), s32[]{:S(2)}) async-start(), calls=%async_computation.12 | async-start | bytes 2359296 | tf_op jit(solution)/shard_map/all_gather | solution.py:18
  7.9 175.0 %all-reduce.9.cloned.1.call-start = ((), (), s32[]{:S(2)}) async-start(), calls=%async_computation.13 | async-start | bytes 8388608
  78.8 0.7 copy-start.8
  78.8 105.9 %copy-start.7 = (s32[2,4]{1,0:T(2,128)S(1)}, s32[2,4]{1,0:T(2,128)}, u32[]{:S(2)}) copy-start(s32[2,4]{1,0:T(2,128)} %param.18) | copy-start | bytes 100
  78.8 131.2 %all-gather.11.cloned.1.call-start = ((), (), s32[]{:S(2)}) async-start(), calls=%async_computation.3 | async-start | bytes 2359296 | tf_op jit(solution)/shard_map/all_gather | solution.py:37
  184.7 78.4 %all-gather.13.cloned.1.call-start = ((), (), s32[]{:S(2)}) async-start(), calls=%async_computation.4 | async-start | bytes 2228224 | tf_op jit(solution)/shard_map/all_gather | solution.py:42
  210.0 7.3 %copy-start.5 = (f32[64,2,512]{2,1,0:T(2,128)S(1)}, f32[64,2,512]{2,1,0:T(2,128)}, u32[]{:S(2)}) copy-start(f32[64,2,512]{2,1,0:T(2,128)} %param.11) | copy-start | bytes 786436
  217.3 72.3 %all-gather.9.cloned.1.call-start = ((), (), s32[]{:S(2)}) async-start(), calls=%async_computation.2 | async-start | bytes 2359296 | tf_op jit(solution)/shard_map/all_gather | solution.py:18
  218.1 139.7 %all-reduce.5.cloned.1.call-start = ((), (), s32[]{:S(2)}) async-start(), calls=%async_computation.5 | async-start | bytes 4194304 | tf_op jit(solution)/shard_map/psum | solution.py:46
  270.1 177.5 %reduce-scatter.3.cloned.1.call-start = ((), (), s32[]{:S(2)}) async-start(), calls=%async_computation.6 | async-start | bytes 4456448 | tf_op jit(solution)/shard_map/reduce_scatter | solution.py:22
  370.0 77.7 %copy-start.6 = (s32[4,2]{0,1:T(2,128)S(1)}, s32[4,2]{0,1:T(2,128)}, u32[]{:S(2)}) copy-start(s32[4,2]{0,1:T(2,128)} %param.19) | copy-start | bytes 100
  370.0 103.7 %all-gather.17.cloned.1.call-start = ((), (), s32[]{:S(2)}) async-start(), calls=%async_computation.8 | async-start | bytes 2359296 | tf_op jit(solution)/shard_map/all_gather | solution.py:37
  447.6 89.6 %all-gather.19.cloned.1.call-start = ((), (), s32[]{:S(2)}) async-start(), calls=%async_computation.9 | async-start | bytes 2228224 | tf_op jit(solution)/shard_map/all_gather | solution.py:42
  482.3 3.0 copy-start.1
  487.7 49.5 %copy-start.3 = (f32[4,256,256]{2,1,0:T(8,128)S(1)}, f32[4,256,256]{2,1,0:T(8,128)}, u32[]{:S(2)}) copy-start(f32[4,256,256]{2,1,0:T(8,128)} %param.17) | copy-start | bytes 3145732
  491.4 72.4 %all-gather.15.cloned.1.call-start = ((), (), s32[]{:S(2)}) async-start(), calls=%async_computation.7 | async-start | bytes 2359296 | tf_op jit(solution)/shard_map/all_gather | solution.py:18
  493.2 139.1 %all-reduce.7.cloned.1.call-start = ((), (), s32[]{:S(2)}) async-start(), calls=%async_computation.10 | async-start | bytes 4194304 | tf_op jit(solution)/shard_map/psum | solution.py:46
  542.0 175.5 %reduce-scatter.5.cloned.1.call-start = ((), (), s32[]{:S(2)}) async-start(), calls=%async_computation.11 | async-start | bytes 4456448 | tf_op jit(solution)/shard_map/reduce_scatter | solution.py:22
  640.0 0.9 copy-start.2
  640.0 1.7 copy-start.4
Sparse Core Ops, SparseCore 0:
  9.7 27.5 all-gather.20
  79.0 103.9 all-reduce.8
  185.2 24.7 all-gather.10
  217.4 45.5 all-gather.12
  265.2 24.3 all-gather.8
  291.8 65.9 all-reduce.4
  370.1 77.3 reduce-scatter.2
  449.4 24.3 all-gather.16
  491.5 45.5 all-gather.18
  539.4 24.3 all-gather.14
  566.3 65.9 all-reduce.6
  640.2 77.3 reduce-scatter.4
where the time goes:
time: 727 us; the launch traced here: 726 us
  waiting for transfers between devices  602 us (83%)
  matrix products  62.3 us (9%)
  local copies, waits for them, and re-layouts  42.2 us (6%)
  between operations  15 us (2%)
    reduce_scatter x2, waiting for transfers between devices, solve_terms(): lax.psum_scatter(jnp.einsum('ski,kij->skj', right_rows, inverse, precisio...  152 us
    psum x2, waiting for transfers between devices, finish_level(): summed = lax.psum(partial_value, 'col')  137 us
    unnamed x13, waiting for transfers between devices  103 us
    all_gather x2, waiting for transfers between devices, fetch_ancestors(): lax.all_gather(pick_blocks(source_rows, blocks), 'wide', axis=0, tiled=True)  88.8 us
    all_gather x3, waiting for transfers between devices, spread_rhs(): return lax.all_gather(local_part, 'col', axis=0, tiled=True)  70.5 us
    all_gather x2, waiting for transfers between devices, spread_solved(): gathered = lax.all_gather(solved_local, 'col', axis=2, tiled=True)  50.9 us
    dot_general x3, matrix products, solve_terms(): jnp.einsum('ski,kij->skj', right_rows, inverse, precision=PRECISE, prefer...  50.4 us
  transfers between devices with their start and end apart: 12, of which 12 were waited for; matrix products, arithmetic and copies ran while one was open for 2% of the time, Pallas kernels for 0%

commit v1 on v0

--- a/solution.py
+++ b/solution.py
@@ -34,7 +34,12 @@
 
 
 def spread_solved(solved_local):
-    gathered = lax.all_gather(solved_local, "col", axis=2, tiled=True)
+    ring = [solved_local]
+    for hop in range(7):
+        ring.append(lax.ppermute(ring[-1], "col", [(dev, (dev + 1) % 8) for dev in range(8)]))
+    gathered = jnp.roll(
+        jnp.concatenate(ring[::-1], axis=2), (lax.axis_index("col") + 1) * ring[0].shape[2], axis=2
+    )
     return gathered.reshape(gathered.shape[0], -1)
 
 

time: 727 us -> 779 us (1.072)
  waiting for transfers between devices: 602 us -> 645 us
  local copies, waits for them, and re-layouts: 42.2 us -> 50.5 us
    ppermute x0 -> x14, waiting for transfers between devices: none -> 98.8 us  [spread_solved(): lax.ppermute(ring[-1], 'col', [(dev, (dev + 1) % 8) for dev in range(8)])]
    all_gather x2 -> x0, waiting for transfers between devices: 50.9 us -> none  [spread_solved(): gathered = lax.all_gather(solved_local, 'col', axis=2, tiled=True)]
    unnamed x28 -> x62, local copies, waits for them, and re-layouts: 9.93 us -> 19 us
    unnamed x13 -> x11, waiting for transfers between devices: 103 us -> 103 us
  transfers between devices with their start and end apart: 12 -> 24, of which waited for: 12 -> 24; matrix products, arithmetic and copies ran while one was open for 2% -> 2% of each run, Pallas kernels for 0% -> 0%
where the time goes in v1:
time: 779 us; the launch traced here: 778 us
  waiting for transfers between devices  645 us (83%)
  matrix products  62.4 us (8%)
  local copies, waits for them, and re-layouts  50.5 us (6%)
  between operations  15.2 us (2%)
    reduce_scatter x2, waiting for transfers between devices, solve_terms(): lax.psum_scatter(jnp.einsum('ski,kij->skj', right_rows, inverse, precisio...  154 us
    psum x2, waiting for transfers between devices, finish_level(): summed = lax.psum(partial_value, 'col')  137 us
    unnamed x11, waiting for transfers between devices  103 us
    ppermute x14, waiting for transfers between devices, spread_solved(): lax.ppermute(ring[-1], 'col', [(dev, (dev + 1) % 8) for dev in range(8)])  98.8 us
    all_gather x2, waiting for transfers between devices, fetch_ancestors(): lax.all_gather(pick_blocks(source_rows, blocks), 'wide', axis=0, tiled=True)  82.2 us
    all_gather x3, waiting for transfers between devices, spread_rhs(): return lax.all_gather(local_part, 'col', axis=0, tiled=True)  70.6 us
    dot_general x3, matrix products, solve_terms(): jnp.einsum('ski,kij->skj', right_rows, inverse, precision=PRECISE, prefer...  50.5 us
    unnamed x62, local copies, waits for them, and re-layouts  19 us
  transfers between devices with their start and end apart: 24, of which 24 were waited for; matrix products, arithmetic and copies ran while one was open for 2% of the time, Pallas kernels for 0%

profile of v1, /device:TPU:0, one launch (start us, length us, event | category | flops | bytes accessed | tf_op | source)
XLA Modules:
  0.0 778.0 jit_solution(8227458931803628697)
XLA Ops:
  8.0 29.4 %all-gather.15.cloned.1.call-done = f32[512,1024]{1,0:T(8,128)} async-done(((f32[64,1024]{1,0:T(8,128)}), f32[512,1024]{1,0:T(8,128)}) %all-gather.15.cloned.1.call-update) | async-done | bytes 2097168 | tf_op jit(solution)/shard_map/all_gather | solution.py:18
  37.4 30.5 %convolution_bitcast_fusion = f32[512,1,2048]{0,2,1:T(8,128)} fusion(f32[1024,2048]{1,0:T(8,128)} %param.13, f32[512,1024]{1,0:T(8,128)} %all-gather.15.cloned.1.call-done), kind=kOutput, calls=%fused_computation.3 | convolution fusion | flops 12884901888 | bytes 14680064 | tf_op jit(solution)/shard_map/ski,kij->skj/dot_general | solution.py:23
  67.8 11.0 %copy.53 = f32[512,1,2048]{2,1,0:T(1,128)} copy(f32[512,1,2048]{0,2,1:T(8,128)} %convolution_bitcast_fusion) | data formatting | bytes 8388608 | tf_op jit(solution)/shard_map/ski,kij->skj/transpose | solution.py:23
  80.8 102.3 %all-reduce.9.cloned.1.call-done = f32[512,1,2048]{2,1,0:T(1,128)} async-done(((f32[512,1,2048]{2,1,0:T(1,128)}), f32[512,1,2048]{2,1,0:T(1,128)}) %all-reduce.9.cloned.1.call-update) | async-done | bytes 4194320
  184.1 7.0 collective-permute-done
  191.1 7.0 collective-permute-done.1
  198.1 7.0 collective-permute-done.2
  205.1 7.0 collective-permute-done.3
  212.1 7.1 collective-permute-done.4
  219.6 6.9 collective-permute-done.5
  226.6 7.2 collective-permute-done.6
  233.8 1.0 constant_dynamic-update-slice_fusion.14
  234.8 1.0 constant_dynamic-update-slice_fusion.13
  236.0 1.0 constant_dynamic-update-slice_fusion.6
  237.0 1.0 constant_dynamic-update-slice_fusion.5
  239.4 2.6 copy.58
  242.0 2.1 gather_fusion
  245.9 41.8 %all-gather.9.cloned.1.call-done = f32[512,2,512]{2,0,1:T(8,128)} async-done(((f32[32,2,512]{2,0,1:T(8,128)}), f32[512,2,512]{2,0,1:T(8,128)}) %all-gather.9.cloned.1.call-update) | async-done | bytes 2097168 | tf_op jit(solution)/shard_map/all_gather | solution.py:47
  287.7 7.1 convolution_bitcast_fusion.4
  294.8 19.4 %all-gather.7.cloned.1.call-done = f32[512,2,512]{2,0,1:T(8,128)} async-done(((f32[64,2,512]{2,0,1:T(8,128)}), f32[512,2,512]{2,0,1:T(8,128)}) %all-gather.7.cloned.1.call-update) | async-done | bytes 2097168 | tf_op jit(solution)/shard_map/all_gather | solution.py:18
  314.2 68.2 %all-reduce.5.cloned.1.call-done = f32[512,2,512]{2,0,1:T(8,128)} async-done(((f32[512,2,512]{2,0,1:T(8,128)}), f32[512,2,512]{2,0,1:T(8,128)}) %all-reduce.5.cloned.1.call-update) | async-done | bytes 2097168 | tf_op jit(solution)/shard_map/psum | solution.py:51
  382.4 12.2 %convolution_bitcast_fusion.2 = f32[512,2,1024]{2,0,1:T(8,128)} fusion(f32[2,512,1024]{2,1,0:T(8,128)} %param.14, f32[512,2,512]{2,0,1:T(8,128)} %all-gather.7.cloned.1.call-done, f32[512,2,512]{2,0,1:T(8,128)} %all-reduce.5.cloned.1.call-done), kind=kOutput, calls=%fused_computation.5 | convolution fusion | flops 6442975232 | bytes 12582912 | tf_op jit(solution)/shard_map/ski,kij->skj/dot_general | solution.py:23
  394.9 77.3 %reduce-scatter.3.cloned.1.call-done = f32[32,2,1024]{2,0,1:T(8,128)} async-done(((f32[512,2,1024]{2,0,1:T(8,128)}), f32[32,2,1024]{2,0,1:T(8,128)}) %reduce-scatter.3.cloned.1.call-update) | async-done | bytes 262160 | tf_op jit(solution)/shard_map/reduce_scatter | solution.py:22
  472.2 7.2 collective-permute-done.7
  479.4 7.0 collective-permute-done.8
  486.5 7.0 collective-permute-done.9
  493.5 7.0 collective-permute-done.10
  500.5 7.0 collective-permute-done.11
  508.2 7.1 collective-permute-done.12
  515.4 7.2 collective-permute-done.13
  523.6 1.0 constant_dynamic-update-slice_fusion.30
  524.6 1.0 constant_dynamic-update-slice_fusion.29
  525.6 1.0 constant_dynamic-update-slice_fusion.24
  526.6 1.0 constant_dynamic-update-slice_fusion.23
  527.6 1.0 constant_dynamic-update-slice_fusion.22
  528.9 3.0 copy.62
  531.9 4.0 concatenate.20
  535.9 3.0 copy.64
  538.9 2.4 pad_maximum_fusion
  541.3 2.7 gather_fusion.1
  546.5 1.7 copy.61
  548.3 40.4 %all-gather.13.cloned.1.call-done = f32[512,4,256]{2,0,1:T(8,128)} async-done(((f32[32,4,256]{2,0,1:T(8,128)}), f32[512,4,256]{2,0,1:T(8,128)}) %all-gather.13.cloned.1.call-update) | async-done | bytes 2097168 | tf_op jit(solution)/shard_map/all_gather | solution.py:47
  588.8 4.9 convolution_bitcast_fusion.3
  593.7 21.8 %all-gather.11.cloned.1.call-done = f32[512,4,256]{2,0,1:T(8,128)} async-done(((f32[64,4,256]{2,0,1:T(8,128)}), f32[512,4,256]{2,0,1:T(8,128)}) %all-gather.11.cloned.1.call-update) | async-done | bytes 2097168 | tf_op jit(solution)/shard_map/all_gather | solution.py:18
  615.5 68.5 %all-reduce.7.cloned.1.call-done = f32[512,4,256]{2,0,1:T(8,128)} async-done(((f32[512,4,256]{2,0,1:T(8,128)}), f32[512,4,256]{2,0,1:T(8,128)}) %all-reduce.7.cloned.1.call-update) | async-done | bytes 2097168 | tf_op jit(solution)/shard_map/psum | solution.py:51
  684.0 7.8 convolution_bitcast_fusion.1
  692.7 76.6 %reduce-scatter.5.cloned.1.call-done = f32[32,4,512]{2,0,1:T(8,128)} async-done(((f32[512,4,512]{2,0,1:T(8,128)}), f32[32,4,512]{2,0,1:T(8,128)}) %reduce-scatter.5.cloned.1.call-update) | async-done | bytes 262160 | tf_op jit(solution)/shard_map/reduce_scatter | solution.py:22
  769.3 1.8 copy.69
  (102 shorter events, 12.7 us)
Async XLA Ops:
  7.2 676.9 %copy-start = (f32[4,256,512]{2,1,0:T(8,128)S(1)}, f32[4,256,512]{2,1,0:T(8,128)}, u32[]{:S(2)}) copy-start(f32[4,256,512]{2,1,0:T(8,128)} %param.15) | copy-start | bytes 6291460
  7.2 30.2 %all-gather.15.cloned.1.call-start = ((), (), s32[]{:S(2)}) async-start(), calls=%async_computation.10 | async-start | bytes 2359296 | tf_op jit(solution)/shard_map/all_gather | solution.py:18
  7.9 175.1 %all-reduce.9.cloned.1.call-start = ((), (), s32[]{:S(2)}) async-start(), calls=%async_computation.11 | async-start | bytes 8388608
  78.9 0.7 copy-start.9
  78.9 140.4 %copy-start.8 = (s32[2,4]{1,0:T(2,128)S(1)}, s32[2,4]{1,0:T(2,128)}, u32[]{:S(2)}) copy-start(s32[2,4]{1,0:T(2,128)} %param.18) | copy-start | bytes 100
  78.9 140.5 %copy-start.7 = (s32[4,2]{0,1:T(2,128)S(1)}, s32[4,2]{0,1:T(2,128)}, u32[]{:S(2)}) copy-start(s32[4,2]{0,1:T(2,128)} %param.19) | copy-start | bytes 100
  78.9 208.8 %all-gather.9.cloned.1.call-start = ((), (), s32[]{:S(2)}) async-start(), calls=%async_computation.3 | async-start | bytes 2228224 | tf_op jit(solution)/shard_map/all_gather | solution.py:47
  184.1 7.0 collective-permute-start
  191.1 7.0 collective-permute-start.1
  198.1 7.0 collective-permute-start.2
  205.1 7.0 collective-permute-start.3
  212.1 7.1 collective-permute-start.4
  219.2 7.3 collective-permute-start.5
  226.6 7.2 collective-permute-start.6
  239.0 6.1 copy-start.6
  245.0 69.2 %all-gather.7.cloned.1.call-start = ((), (), s32[]{:S(2)}) async-start(), calls=%async_computation.2 | async-start | bytes 2359296 | tf_op jit(solution)/shard_map/all_gather | solution.py:18
  245.8 136.5 %all-reduce.5.cloned.1.call-start = ((), (), s32[]{:S(2)}) async-start(), calls=%async_computation.4 | async-start | bytes 4194304 | tf_op jit(solution)/shard_map/psum | solution.py:51
  294.8 177.5 %reduce-scatter.3.cloned.1.call-start = ((), (), s32[]{:S(2)}) async-start(), calls=%async_computation.5 | async-start | bytes 4456448 | tf_op jit(solution)/shard_map/reduce_scatter | solution.py:22
  394.6 194.1 %all-gather.13.cloned.1.call-start = ((), (), s32[]{:S(2)}) async-start(), calls=%async_computation.7 | async-start | bytes 2228224 | tf_op jit(solution)/shard_map/all_gather | solution.py:47
  472.2 56.5 %copy-start.2 = (f32[32,2,1024]{2,0,1:T(8,128)S(1)}, f32[32,2,1024]{2,0,1:T(8,128)}, u32[]{:S(2)}) copy-start(f32[32,2,1024]{2,0,1:T(8,128)} %reduce-scatter.3.cloned.1.call-done) | copy-start | bytes 786436
  472.2 7.2 collective-permute-start.7
  479.4 7.0 collective-permute-start.8
  486.5 7.0 collective-permute-start.9
  493.5 7.0 collective-permute-start.10
  500.5 7.0 collective-permute-start.11
  507.5 0.7 copy-start.4
  508.2 7.1 collective-permute-start.12
  515.3 7.3 collective-permute-start.13
  515.3 13.2 %copy-start.5 = (f32[32,2,1024]{2,0,1:T(8,128)S(1)}, f32[32,2,1024]{2,0,1:T(8,128)}, u32[]{:S(2)}) copy-start(f32[32,2,1024]{2,0,1:T(8,128)} %copy-done.4) | copy-start | bytes 786436
  535.9 3.0 copy-start.1
  538.9 49.9 %copy-start.3 = (f32[4,256,256]{2,1,0:T(8,128)S(1)}, f32[4,256,256]{2,1,0:T(8,128)}, u32[]{:S(2)}) copy-start(f32[4,256,256]{2,1,0:T(8,128)} %param.17) | copy-start | bytes 3145732
  546.5 69.0 %all-gather.11.cloned.1.call-start = ((), (), s32[]{:S(2)}) async-start(), calls=%async_computation.6 | async-start | bytes 2359296 | tf_op jit(solution)/shard_map/all_gather | solution.py:18
  548.3 135.7 %all-reduce.7.cloned.1.call-start = ((), (), s32[]{:S(2)}) async-start(), calls=%async_computation.8 | async-start | bytes 4194304 | tf_op jit(solution)/shard_map/psum | solution.py:51
  593.7 175.6 %reduce-scatter.5.cloned.1.call-start = ((), (), s32[]{:S(2)}) async-start(), calls=%async_computation.9 | async-start | bytes 4456448 | tf_op jit(solution)/shard_map/reduce_scatter | solution.py:22
Sparse Core Ops, SparseCore 0:
  9.7 27.5 all-gather.14
  79.0 103.9 all-reduce.8
  245.1 42.5 all-gather.8
  289.8 24.3 all-gather.6
  316.4 65.9 all-reduce.4
  394.8 77.4 reduce-scatter.2
  546.6 42.0 all-gather.12
  591.1 24.3 all-gather.10
  618.0 65.9 all-reduce.6
  691.9 77.3 reduce-scatter.4
